TPU v7x, 128 devices: a whole 4x4x4 slice. The times are simulated.
128 devices in a mesh: rep: 64 (over z, y, x_hi, core), shard: 2 (over x_lo).
Axes of the slice: x: 4 (x_hi: 2, x_lo: 2; x = x_hi * 2 + x_lo), y: 4, z: 4, core: 2. Of those that a mesh axis runs over, the one named last changes fastest.
Arguments:
- grad_xproj: bfloat16 [256, 2, 3072, 128], P(('rep', 'shard')), may hold values from -32 to 32
- grad_chan: bfloat16 [256, 2, 118, 3072], P(('rep', 'shard')), may hold values from -32 to 32
- grad_embed: bfloat16 [256, 1024, 1536], P(('rep', 'shard')), may hold values from -32 to 32
- weight_xproj: float32 [2, 3072, 128], P(None, 'shard'), may hold values from -0.3125 to 0.3125
- weight_chan: float32 [2, 118, 3072], P(None, None, 'shard'), may hold values from -0.3125 to 0.3125
- weight_embed: float32 [1024, 1536], P('shard'), may hold values from -0.3125 to 0.3125
- moment_xproj: float32 [2, 3072, 128], P(None, 'shard'), may hold values from -0.015625 to 0.015625
- moment_chan: float32 [2, 118, 3072], P(None, None, 'shard'), may hold values from -0.015625 to 0.015625
- moment_embed: float32 [1024, 1536], P('shard'), may hold values from -0.015625 to 0.015625
- second_xproj: float32 [2, 3072, 128], P(None, 'shard'), may hold values from 1e-08 to 1e-05
- second_chan: float32 [2, 118, 3072], P(None, None, 'shard'), may hold values from 1e-08 to 1e-05
- second_embed: float32 [1024, 1536], P('shard'), may hold values from 1e-08 to 1e-05
Outputs:
- new_weight_xproj: float32 [2, 3072, 128], P(None, 'shard')
- new_weight_chan: float32 [2, 118, 3072], P(None, None, 'shard')
- new_weight_embed: float32 [1024, 1536], P('shard')
- new_moment_xproj: float32 [2, 3072, 128], P(None, 'shard')
- new_moment_chan: float32 [2, 118, 3072], P(None, None, 'shard')
- new_moment_embed: float32 [1024, 1536], P('shard')
- new_second_xproj: float32 [2, 3072, 128], P(None, 'shard')
- new_second_chan: float32 [2, 118, 3072], P(None, None, 'shard')
- new_second_embed: float32 [1024, 1536], P('shard')
- full_xproj: bfloat16 [2, 3072, 128], replicated
- full_chan: bfloat16 [2, 118, 3072], replicated
- full_embed: bfloat16 [1024, 1536], replicated
- pre_norm: float32 [1], replicated
All inputs are finite; a program needn't handle non-finite values.
Results may differ from a plain program's by a relative error of at most 0.00085.
Values may be sent and summed in bfloat16 or wider, within the bound.
No kernel may reach another device: no remote copies, remote signals or barrier semaphores. Data moves between devices by JAX's collectives and lax.ppermute only.
A program may use at most 448 MiB of HBM per device.

v0:
```python
import jax
import jax.numpy as jnp
from jax import lax
from jax.sharding import PartitionSpec as P

beta_one = 0.9
beta_two = 0.999
learn_rate = 0.003
decay_rate = 0.1
epsilon = 1e-08
correct_one = 0.9999734386011124
correct_two = 0.09520785288629094


def adamw_update(weight, moment, second, gradient, clip_factor):
    clipped = clip_factor * gradient
    new_moment = beta_one * moment + (1.0 - beta_one) * clipped
    new_second = beta_two * second + (1.0 - beta_two) * clipped * clipped
    step_size = new_moment / correct_one / (jnp.sqrt(new_second / correct_two) + epsilon)
    new_weight = weight - learn_rate * (step_size + decay_rate * weight)
    return (new_weight, new_moment, new_second)


def on_device(
    grad_xproj,
    grad_chan,
    grad_embed,
    weight_xproj,
    weight_chan,
    weight_embed,
    moment_xproj,
    moment_chan,
    moment_embed,
    second_xproj,
    second_chan,
    second_embed,
):
    count_rep = lax.axis_size("rep")
    count_shard = lax.axis_size("shard")
    micro, layers, inner, xw = grad_xproj.shape
    _, _, ch, _ = grad_chan.shape
    gx = grad_xproj.reshape(micro, layers, count_shard, inner // count_shard, xw)
    summed_x = jnp.transpose(jnp.sum(gx, axis=0, dtype=jnp.float32), (1, 0, 2, 3))
    gc = grad_chan.reshape(micro, layers, ch, count_shard, inner // count_shard)
    summed_c = jnp.transpose(jnp.sum(gc, axis=0, dtype=jnp.float32), (2, 0, 1, 3))
    summed_e = jnp.sum(grad_embed, axis=0, dtype=jnp.float32)
    part_x = lax.psum_scatter(
        summed_x.astype(jnp.bfloat16), "shard", scatter_dimension=0, tiled=True
    )
    part_c = lax.psum_scatter(
        summed_c.astype(jnp.bfloat16), "shard", scatter_dimension=0, tiled=True
    )
    part_e = lax.psum_scatter(
        summed_e.astype(jnp.bfloat16), "shard", scatter_dimension=0, tiled=True
    )
    block_x = lax.psum(part_x, "rep")[0]
    block_c = lax.psum(part_c, "rep")[0]
    block_e = lax.psum(part_e, "rep")
    inverse = 1.0 / (micro * count_rep * count_shard)
    mean_x = block_x.astype(jnp.float32) * inverse
    mean_c = block_c.astype(jnp.float32) * inverse
    mean_e = block_e.astype(jnp.float32) * inverse
    partial_squares = jnp.sum(mean_x * mean_x) + jnp.sum(mean_c * mean_c) + jnp.sum(mean_e * mean_e)
    squares = lax.psum(partial_squares, "shard")
    norm_value = jnp.sqrt(squares)
    clip_factor = jnp.minimum(1.0, 1.0 / (norm_value + 1e-06))
    wx, mx, vx = adamw_update(weight_xproj, moment_xproj, second_xproj, mean_x, clip_factor)
    wc, mc, vc = adamw_update(weight_chan, moment_chan, second_chan, mean_c, clip_factor)
    we, me, ve = adamw_update(weight_embed, moment_embed, second_embed, mean_e, clip_factor)
    gathered = (
        lax.all_gather(wx.astype(jnp.bfloat16), "shard", axis=1, tiled=True),
        lax.all_gather(wc.astype(jnp.bfloat16), "shard", axis=2, tiled=True),
        lax.all_gather(we.astype(jnp.bfloat16), "shard", axis=0, tiled=True),
    )
    return (
        wx,
        wc,
        we,
        mx,
        mc,
        me,
        vx,
        vc,
        ve,
        gathered[0],
        gathered[1],
        gathered[2],
        jnp.reshape(norm_value, (1,)),
    )


def solution(mesh):
    placed = (
        P(("rep", "shard"), None, None, None),
        P(("rep", "shard"), None, None, None),
        P(("rep", "shard"), None, None),
        P(None, "shard", None),
        P(None, None, "shard"),
        P("shard", None),
        P(None, "shard", None),
        P(None, None, "shard"),
        P("shard", None),
        P(None, "shard", None),
        P(None, None, "shard"),
        P("shard", None),
    )
    return jax.shard_map(
        on_device,
        mesh=mesh,
        in_specs=placed,
        out_specs=(
            P(None, "shard", None),
            P(None, None, "shard"),
            P("shard", None),
            P(None, "shard", None),
            P(None, None, "shard"),
            P("shard", None),
            P(None, "shard", None),
            P(None, None, "shard"),
            P("shard", None),
            P(),
            P(),
            P(),
            P(),
        ),
        check_vma=False,
    )
```

profile of v0, /device:TPU:1, one launch (start us, length us, event | category | flops | bytes accessed | tf_op | source)
XLA Modules:
  0.0 956.5 jit_solution(9110890464267347480)
XLA Ops:
  7.2 0.0 all-reduce.9.cloned.1.call-start
  7.2 6.5 reduce_sum.65
  13.7 1.0 reshape.52
  14.7 2.2 copy.42
  16.9 4.0 reduce_sum.63
  20.9 0.0 all-reduce.9.cloned.1.call-update
  20.9 0.0 reduce-scatter.5.cloned.1.call-start
  21.0 6.5 reduce_sum.67
  27.5 0.0 reduce-scatter.5.cloned.1.call-update
  27.5 0.0 all-reduce.7.cloned.1.call-start
  27.6 0.6 copy-done.6
  28.1 0.6 dynamic-slice
  28.7 85.4 %all-reduce.9.cloned.1.call-done = (bf16[2,2,1536,128]{3,2,0,1:T(8,128)(2,1)}, bf16[2,2,118,1536]{3,1,2,0:T(2,128)(2,1)}) async-done(((bf16[2,2,1536,128]{3,2,0,1:T(8,128)(2,1)}, bf16[2,2,118,1536]{3,1,2,0:T(2,128)(2,1)}), (bf16[2,2,1536,128]{3,2,0,1:T(8,128)(2,1)}, bf16[2,2,118,1536]{3,1,2,0:T(2,128)(2,1)})) %all-reduce.9.cloned.1.call-update) | async-done | bytes 3022864
  114.2 2.4 constant_dynamic-slice_fusion
  116.5 0.9 copy.43
  117.5 0.0 copy-done.5
  117.5 1.6 constant_dynamic-slice_fusion.1
  119.1 45.0 %reduce-scatter.5.cloned.1.call-done = bf16[512,1536]{1,0:T(8,128)(2,1)} async-done(((bf16[1024,1536]{1,0:T(8,128)(2,1)}), bf16[512,1536]{1,0:T(8,128)(2,1)}) %reduce-scatter.5.cloned.1.call-update) | async-done | bytes 1572880 | tf_op jit(solution)/shard_map/reduce_scatter | solution.py:53
  164.1 0.0 all-reduce.7.cloned.1.call-update
  164.1 0.2 all-gather.6.cloned.1.call-start
  164.3 647.6 %all-reduce.7.cloned.1.call-done = (bf16[1,2,1536,128]{3,2,0,1:T(8,128)(2,1)}, bf16[1,2,118,1536]{3,2,1,0:T(8,128)(2,1)}, bf16[512,1536]{1,0:T(8,128)(2,1)}) async-done(((bf16[1,2,1536,128]{3,2,0,1:T(8,128)(2,1)}, bf16[1,2,118,1536]{3,2,1,0:T(8,128)(2,1)}, bf16[512,1536]{1,0:T(8,128)(2,1)}), (bf16[1,2,1536,128]{3,2,0,1:T(8,128)(2,1)}, bf16[1,2,118,1536]{3,2,1,0:T(8,128)(2,1)}, ...) | async-done | bytes 3084304 | tf_op jit(solution)/shard_map/psum | solution.py:56
  812.0 2.2 fusion.12
  814.1 2.1 fusion.6
  816.3 2.8 fusion.3
  821.0 4.3 psum.31
  826.1 0.0 copy-done.4
  826.1 5.5 fusion.20
  831.6 0.0 all-gather.6.cloned.1.call-update
  831.6 0.0 all-gather.4.cloned.1.call-start
  831.7 0.0 copy-start
  831.7 6.0 fusion.23
  837.7 0.0 all-gather.4.cloned.1.call-update
  837.8 0.0 all-gather.8.cloned.1.call-start
  837.8 0.0 copy-done
  837.8 7.3 fusion.17
  845.1 0.0 all-gather.8.cloned.1.call-update
  845.1 0.0 copy-start.1
  845.2 1.3 copy-done.2
  846.5 2.2 copy.48
  848.7 0.0 copy-done.1
  848.7 2.2 copy.49
  850.9 2.2 copy.50
  853.2 8.0 all-gather.6.cloned.1.call-done
  861.1 4.0 copy.51
  865.1 28.4 %all-gather.4.cloned.1.call-done = bf16[2,3072,128]{2,1,0:T(8,128)(2,1)} async-done(((bf16[2,1536,128]{2,1,0:T(8,128)(2,1)}), bf16[2,3072,128]{2,1,0:T(8,128)(2,1)}) %all-gather.4.cloned.1.call-update) | async-done | bytes 1572880 | tf_op jit(solution)/shard_map/all_gather | solution.py:71
  893.4 50.6 %all-gather.8.cloned.1.call-done = bf16[1024,1536]{1,0:T(8,128)(2,1)} async-done(((bf16[512,1536]{1,0:T(8,128)(2,1)}), bf16[1024,1536]{1,0:T(8,128)(2,1)}) %all-gather.8.cloned.1.call-update) | async-done | bytes 3145744 | tf_op jit(solution)/shard_map/all_gather | solution.py:73
  944.1 2.8 copy.73
  946.9 1.7 copy.74
  (6 shorter events, 0.0 us)
Async XLA Ops:
  7.2 107.0 %all-reduce.9.cloned.1.call-start = ((), (), s32[]{:S(2)}) async-start(), calls=%async_computation.6 | async-start | bytes 6045696
  20.9 143.1 %reduce-scatter.5.cloned.1.call-start = ((), (), s32[]{:S(2)}) async-start(), calls=%async_computation.1 | async-start | bytes 4718592 | tf_op jit(solution)/shard_map/reduce_scatter | solution.py:53
  27.5 0.7 copy-start.6
  27.5 784.4 %all-reduce.7.cloned.1.call-start = ((), (), s32[]{:S(2)}) async-start(), calls=%async_computation.5 | async-start | bytes 6193152 | tf_op jit(solution)/shard_map/psum | solution.py:56
  114.1 3.3 copy-start.5
  164.1 697.0 %all-gather.6.cloned.1.call-start = ((), (), s32[]{:S(2)}) async-start(), calls=%async_computation.3 | async-start | bytes 2211840 | tf_op jit(solution)/shard_map/all_gather | solution.py:72
  811.9 14.1 %copy-start.4 = (bf16[1,2,118,1536]{3,2,1,0:T(8,128)(2,1)S(1)}, bf16[1,2,118,1536]{3,2,1,0:T(8,128)(2,1)}, u32[]{:S(2)}) copy-start(bf16[1,2,118,1536]{3,2,1,0:T(8,128)(2,1)} %get-tuple-element.53) | copy-start | bytes 2174980
  831.6 61.8 %all-gather.4.cloned.1.call-start = ((), (), s32[]{:S(2)}) async-start(), calls=%async_computation.2 | async-start | bytes 2359296 | tf_op jit(solution)/shard_map/all_gather | solution.py:71
  831.7 6.1 copy-start
  837.8 106.3 %all-gather.8.cloned.1.call-start = ((), (), s32[]{:S(2)}) async-start(), calls=%async_computation.4 | async-start | bytes 4718592 | tf_op jit(solution)/shard_map/all_gather | solution.py:73
  845.1 1.4 copy-start.2
  845.1 3.6 copy-start.1
  944.1 2.8 copy-start.3
Sparse Core Ops, SparseCore 0:
  21.1 93.0 all-reduce.8
  117.2 46.8 reduce-scatter.4
  167.9 643.9 all-reduce.6
  831.8 29.3 all-gather.5
  862.7 30.6 all-gather.3
  895.6 48.4 all-gather.7
where the time goes:
time: 957 us
  waiting for transfers between devices  865 us (90%)
  other arithmetic  43 us (4%)
  local copies, waits for them, and re-layouts  25.7 us (3%)
  between operations  18 us (2%)
    psum x1, waiting for transfers between devices, on_device(): block_x = lax.psum(part_x, 'rep')[0]  648 us
    unnamed x7, waiting for transfers between devices  85.5 us
    all_gather x1, waiting for transfers between devices, on_device(): lax.all_gather(we.astype(jnp.bfloat16), 'shard', axis=0, tiled=True)  50.6 us
    reduce_scatter x1, waiting for transfers between devices, on_device(): lax.psum_scatter(summed_e.astype(jnp.bfloat16), 'shard', scatter_dimensio...  45 us
    all_gather x1, waiting for transfers between devices, on_device(): lax.all_gather(wx.astype(jnp.bfloat16), 'shard', axis=1, tiled=True)  28.4 us
    unnamed x23, local copies, waits for them, and re-layouts  21.6 us
  transfers between devices with their start and end apart: 6, of which 6 were waited for; matrix products, arithmetic and copies ran while one was open for 4% of the time, Pallas kernels for 0%

commit v1 on v0

--- a/solution.py
+++ b/solution.py
@@ -10,6 +10,12 @@
 epsilon = 1e-08
 correct_one = 0.9999734386011124
 correct_two = 0.09520785288629094
+
+
+def add_all(shard, mesh_axis):
+    pieces = lax.all_gather(shard, mesh_axis, axis=0, tiled=False)
+    total = pieces.sum(axis=0)
+    return total
 
 
 def adamw_update(weight, moment, second, gradient, clip_factor):
@@ -53,7 +59,7 @@
     part_e = lax.psum_scatter(
         summed_e.astype(jnp.bfloat16), "shard", scatter_dimension=0, tiled=True
     )
-    block_x = lax.psum(part_x, "rep")[0]
+    block_x = add_all(part_x, "rep")[0]
     block_c = lax.psum(part_c, "rep")[0]
     block_e = lax.psum(part_e, "rep")
     inverse = 1.0 / (micro * count_rep * count_shard)

time: 957 us -> 1170 us (1.22)
  waiting for transfers between devices: 865 us -> 1060 us
  other arithmetic: 43 us -> 58.3 us
    all_gather x0 -> x1, waiting for transfers between devices: none -> 210 us  [add_all(): pieces = lax.all_gather(shard, mesh_axis, axis=0, tiled=False)]
    reduce_sum x0 -> x1, other arithmetic: none -> 16.3 us  [add_all(): total = pieces.sum(axis=0)]
    psum x1, waiting for transfers between devices: 648 us -> 634 us  [on_device(): block_c = lax.psum(part_c, 'rep')[0]]
    unnamed x7 -> x8, waiting for transfers between devices: 85.5 us -> 85.5 us
  transfers between devices with their start and end apart: 6 -> 7, of which waited for: 6 -> 7; matrix products, arithmetic and copies ran while one was open for 4% -> 4% of each run, Pallas kernels for 0% -> 0%
where the time goes in v1:
time: 1170 us
  waiting for transfers between devices  1060 us (91%)
  other arithmetic  58.3 us (5%)
  local copies, waits for them, and re-layouts  25.6 us (2%)
  between operations  18 us (2%)
    psum x1, waiting for transfers between devices, on_device(): block_c = lax.psum(part_c, 'rep')[0]  634 us
    all_gather x1, waiting for transfers between devices, add_all(): pieces = lax.all_gather(shard, mesh_axis, axis=0, tiled=False)  210 us
    unnamed x8, waiting for transfers between devices  85.5 us
    all_gather x1, waiting for transfers between devices, on_device(): lax.all_gather(we.astype(jnp.bfloat16), 'shard', axis=0, tiled=True)  50.8 us
    reduce_scatter x1, waiting for transfers between devices, on_device(): lax.psum_scatter(summed_e.astype(jnp.bfloat16), 'shard', scatter_dimensio...  46.7 us
    all_gather x1, waiting for transfers between devices, on_device(): lax.all_gather(wx.astype(jnp.bfloat16), 'shard', axis=1, tiled=True)  28.4 us
  transfers between devices with their start and end apart: 7, of which 7 were waited for; matrix products, arithmetic and copies ran while one was open for 4% of the time, Pallas kernels for 0%

profile of v1, /device:TPU:1, one launch (start us, length us, event | category | flops | bytes accessed | tf_op | source)
XLA Modules:
  0.0 1167.4 jit_solution(2826126833627851653)
XLA Ops:
  7.2 0.0 all-reduce.9.cloned.1.call-start
  7.2 6.5 reduce_sum.78
  13.7 1.0 reshape.50
  14.7 2.2 copy.42
  16.9 4.0 reduce_sum.75
  20.9 0.0 all-reduce.9.cloned.1.call-update
  20.9 0.0 reduce-scatter.5.cloned.1.call-start
  21.0 6.5 reduce_sum.80
  27.5 0.0 reduce-scatter.5.cloned.1.call-update
  27.5 0.0 all-reduce.7.cloned.1.call-start
  27.6 0.6 copy-done.8
  28.1 0.6 dynamic-slice
  28.7 85.4 %all-reduce.9.cloned.1.call-done = (bf16[2,2,1536,128]{3,2,0,1:T(8,128)(2,1)}, bf16[2,2,118,1536]{3,1,2,0:T(2,128)(2,1)}) async-done(((bf16[2,2,1536,128]{3,2,0,1:T(8,128)(2,1)}, bf16[2,2,118,1536]{3,1,2,0:T(2,128)(2,1)}), (bf16[2,2,1536,128]{3,2,0,1:T(8,128)(2,1)}, bf16[2,2,118,1536]{3,1,2,0:T(2,128)(2,1)})) %all-reduce.9.cloned.1.call-update) | async-done | bytes 3022864
  114.1 2.3 constant_dynamic-slice_fusion
  116.4 0.0 copy-start.7
  116.4 0.9 copy.43
  117.4 46.7 %reduce-scatter.5.cloned.1.call-done = bf16[512,1536]{1,0:T(8,128)(2,1)} async-done(((bf16[1024,1536]{1,0:T(8,128)(2,1)}), bf16[512,1536]{1,0:T(8,128)(2,1)}) %reduce-scatter.5.cloned.1.call-update) | async-done | bytes 1572880 | tf_op jit(solution)/shard_map/reduce_scatter | solution.py:59
  164.1 0.0 all-reduce.7.cloned.1.call-update
  164.1 0.0 all-gather.12.cloned.1.call-start
  164.1 0.0 copy-done.7
  164.1 1.6 constant_dynamic-slice_fusion.1
  165.7 0.0 all-gather.12.cloned.1.call-update
  165.8 0.2 all-gather.8.cloned.1.call-start
  166.0 633.7 %all-reduce.7.cloned.1.call-done = (bf16[1,2,118,1536]{3,2,1,0:T(8,128)(2,1)}, bf16[512,1536]{1,0:T(8,128)(2,1)}) async-done(((bf16[1,2,118,1536]{3,2,1,0:T(8,128)(2,1)}, bf16[512,1536]{1,0:T(8,128)(2,1)}), (bf16[1,2,118,1536]{3,2,1,0:T(8,128)(2,1)}, bf16[512,1536]{1,0:T(8,128)(2,1)})) %all-reduce.7.cloned.1.call-update) | async-done | bytes 2297872 | tf_op jit(solution)/shard_map/psum | solution.py:63
  799.7 2.1 fusion.11
  801.8 2.8 fusion.3
  804.6 210.5 %all-gather.12.cloned.1.call-done = bf16[64,2,1536,128]{3,2,0,1:T(8,128)(2,1)} async-done(((bf16[1,2,1536,128]{3,2,0,1:T(8,128)(2,1)}), bf16[64,2,1536,128]{3,2,0,1:T(8,128)(2,1)}) %all-gather.12.cloned.1.call-update) | async-done | bytes 50331664 | tf_op jit(solution)/shard_map/all_gather | solution.py:16
  1015.1 16.3 %reduce.8 = bf16[2,1536,128]{2,1,0:T(8,128)(2,1)S(1)} reduce(bf16[64,2,1536,128]{3,2,0,1:T(8,128)(2,1)} %all-gather.12.cloned.1.call-done, bf16[]{:T(256)} %constant.14.clone.1), dimensions={0}, to_apply=%region_2.0 | reduce | flops 24772608 | bytes 51118080 | tf_op jit(solution)/shard_map/reduce_sum | solution.py:17
  1031.4 1.0 fusion.8
  1034.4 4.3 psum.23
  1039.4 5.3 fusion.19
  1044.7 0.0 all-gather.8.cloned.1.call-update
  1044.7 0.0 all-gather.6.cloned.1.call-start
  1044.8 5.8 fusion.22
  1050.6 0.0 all-gather.6.cloned.1.call-update
  1050.6 0.0 all-gather.10.cloned.1.call-start
  1050.6 8.0 fusion.16
  1058.7 0.0 all-gather.10.cloned.1.call-update
  1058.7 1.3 copy-done.3
  1060.1 2.2 copy.48
  1062.3 2.2 copy.49
  1064.5 2.2 copy.50
  1066.7 5.1 all-gather.8.cloned.1.call-done
  1071.8 4.0 copy.51
  1075.8 28.4 %all-gather.6.cloned.1.call-done = bf16[2,3072,128]{2,1,0:T(8,128)(2,1)} async-done(((bf16[2,1536,128]{2,1,0:T(8,128)(2,1)}), bf16[2,3072,128]{2,1,0:T(8,128)(2,1)}) %all-gather.6.cloned.1.call-update) | async-done | bytes 1572880 | tf_op jit(solution)/shard_map/all_gather | solution.py:77
  1104.2 50.8 %all-gather.10.cloned.1.call-done = bf16[1024,1536]{1,0:T(8,128)(2,1)} async-done(((bf16[512,1536]{1,0:T(8,128)(2,1)}), bf16[1024,1536]{1,0:T(8,128)(2,1)}) %all-gather.10.cloned.1.call-update) | async-done | bytes 3145744 | tf_op jit(solution)/shard_map/all_gather | solution.py:79
  1154.9 2.8 copy.72
  1157.7 1.7 copy.73
  (14 shorter events, 0.0 us)
Async XLA Ops:
  7.2 107.0 %all-reduce.9.cloned.1.call-start = ((), (), s32[]{:S(2)}) async-start(), calls=%async_computation.7 | async-start | bytes 6045696
  20.9 143.1 %reduce-scatter.5.cloned.1.call-start = ((), (), s32[]{:S(2)}) async-start(), calls=%async_computation.1 | async-start | bytes 4718592 | tf_op jit(solution)/shard_map/reduce_scatter | solution.py:59
  27.5 0.7 copy-start.8
  27.5 772.2 %all-reduce.7.cloned.1.call-start = ((), (), s32[]{:S(2)}) async-start(), calls=%async_computation.6 | async-start | bytes 4620288 | tf_op jit(solution)/shard_map/psum | solution.py:63
  116.4 47.7 %copy-start.7 = (bf16[2,2,1536,128]{3,2,0,1:T(8,128)(2,1)S(1)}, bf16[2,2,1536,128]{3,2,0,1:T(8,128)(2,1)}, u32[]{:S(2)}) copy-start(bf16[2,2,1536,128]{3,2,0,1:T(8,128)(2,1)} %get-tuple-element.54) | copy-start | bytes 4718596
  164.1 851.0 %all-gather.12.cloned.1.call-start = ((), (), s32[]{:S(2)}) async-start(), calls=%async_computation.5 | async-start | bytes 51118080 | tf_op jit(solution)/shard_map/all_gather | solution.py:16
  165.8 906.1 %all-gather.8.cloned.1.call-start = ((), (), s32[]{:S(2)}) async-start(), calls=%async_computation.3 | async-start | bytes 2211840 | tf_op jit(solution)/shard_map/all_gather | solution.py:78
  804.6 234.8 %copy-start.5 = (bf16[1,2,118,1536]{3,2,1,0:T(8,128)(2,1)S(1)}, bf16[1,2,118,1536]{3,2,1,0:T(8,128)(2,1)}, u32[]{:S(2)}) copy-start(bf16[1,2,118,1536]{3,2,1,0:T(8,128)(2,1)} %get-tuple-element.52) | copy-start | bytes 2174980
  1015.1 24.3 %copy-start.6 = (f32[2,118,1536]{2,0,1:T(2,128)S(1)}, f32[2,118,1536]{2,0,1:T(2,128)}, u32[]{:S(2)}) copy-start(f32[2,118,1536]{2,0,1:T(2,128)} %param.16) | copy-start | bytes 4349956
  1044.7 59.4 %all-gather.6.cloned.1.call-start = ((), (), s32[]{:S(2)}) async-start(), calls=%async_computation.2 | async-start | bytes 2359296 | tf_op jit(solution)/shard_map/all_gather | solution.py:77
  1044.8 5.9 copy-start
  1050.6 104.4 %all-gather.10.cloned.1.call-start = ((), (), s32[]{:S(2)}) async-start(), calls=%async_computation.4 | async-start | bytes 4718592 | tf_op jit(solution)/shard_map/all_gather | solution.py:79
  1058.7 1.4 copy-start.3
  1058.7 3.6 copy-start.2
  1062.3 2.2 copy-start.1
  1154.9 2.8 copy-start.4
Sparse Core Ops, SparseCore 0:
  21.1 93.0 all-reduce.8
  117.2 46.8 reduce-scatter.4
  167.2 632.4 all-reduce.6
  804.1 210.9 all-gather.11
  1044.9 26.9 all-gather.7
  1073.4 30.6 all-gather.5
  1106.5 48.4 all-gather.9
